TPU v7x, 256 devices: a whole 4x4x8 slice. The times are simulated.
256 devices in a mesh: section: 32 (over z_hi, y, core), tensor: 8 (over z_lo, x).
Axes of the slice: x: 4, y: 4, z: 8 (z_hi: 4, z_lo: 2; z = z_hi * 2 + z_lo), core: 2. Of those that a mesh axis runs over, the one named last changes fastest.
Arguments:
- acts: bfloat16 [32, 512, 3072], P('section', 'tensor'), may hold values from -6 to 6
- sides: bfloat16 [32, 512, 3072], P('section', 'tensor'), may hold values from -6 to 6
- gains: float32 [32, 3072], P('section'), may hold values from 0.1 to 1.9
- weights: bfloat16 [32, 6144, 3072], P('section', None, 'tensor'), may hold values from -0.078125 to 0.078125
- back_acts: bfloat16 [32, 512, 3072], P('section', 'tensor'), may hold values from -6 to 6
- back_sides: bfloat16 [32, 512, 3072], P('section', 'tensor'), may hold values from -6 to 6
- back_grads: bfloat16 [32, 512, 3072], P('section', 'tensor'), may hold values from -6 to 6
Outputs:
- received: bfloat16 [32, 512, 3072], P('section', 'tensor')
- mirrored: bfloat16 [32, 512, 3072], P('section', 'tensor')
- grad_received: bfloat16 [32, 512, 3072], P('section', 'tensor')
- weight_grads: bfloat16 [32, 6144, 3072], P('section', None, 'tensor')
- gain_grads: float32 [32, 3072], P('section')
All inputs are finite; a program needn't handle non-finite values.
Results may differ from a plain program's by a relative error of at most 0.015.
Values may be sent and summed in bfloat16 or wider, within the bound.
No kernel may reach another device: no remote copies, remote signals or barrier semaphores. Data moves between devices by JAX's collectives and lax.ppermute only.
A program may use at most 128 MiB of HBM per device.

v0:
```python
import jax
import jax.numpy as jnp
from jax import lax
from jax.sharding import PartitionSpec as P

epsilon = 1e-06
tanh_scale = 0.7978845608028654
cubic_term = 0.044715


def swapped(block, axis, apart):
    count = lax.axis_size(axis)
    route = []
    for low in range(count):
        high = low | 1 << apart
        if high != low and high < count:
            route += [(low, high), (high, low)]
    return lax.ppermute(block, axis, route)


def shifted(block, axis, distance):
    devices = range(lax.axis_size(axis))
    route = [((i - distance) % len(devices), i) for i in devices]
    return lax.ppermute(block, axis, route)


def gelu_value(inputs):
    inside = tanh_scale * (inputs + cubic_term * inputs * inputs * inputs)
    return 0.5 * inputs * (1.0 + jnp.tanh(inside))


def gelu_slope(inputs):
    inside = tanh_scale * (inputs + cubic_term * inputs * inputs * inputs)
    bent = jnp.tanh(inside)
    return 0.5 * (1.0 + bent) + 0.5 * inputs * (1.0 - bent * bent) * tanh_scale * (
        1.0 + 3.0 * cubic_term * inputs * inputs
    )


def normalize(rows_in, gain):
    xfloat = rows_in.astype(jnp.float32)
    rinv = lax.rsqrt(jnp.mean(xfloat * xfloat, axis=-1, keepdims=True) + epsilon)
    return (xfloat, rinv, (xfloat * rinv * gain).astype(jnp.bfloat16))


def mirror(payload):
    sections = lax.axis_size("section")
    levels = sections.bit_length() - 1
    for bit_idx in range(levels):
        payload = swapped(payload, "section", bit_idx)
    return payload


def on_device(acts, sides, gains, weights, back_acts, back_sides, back_grads):
    sections = lax.axis_size("section")
    middle = sections // 2
    section_idx = lax.axis_index("section")
    gain = gains[0]
    weight_all = weights[0]
    rows, width = acts[0].shape
    w_top = weight_all[:width]
    w_bottom = weight_all[width:]
    xfloat, rinv, normed = normalize(acts[0], gain)
    normed_all, side_all = (
        lax.all_gather(normed, "tensor", axis=0, tiled=True),
        lax.all_gather(sides[0], "tensor", axis=0, tiled=True),
    )
    hidden = jnp.dot(normed_all, w_top, preferred_element_type=jnp.float32) + jnp.dot(
        side_all, w_bottom, preferred_element_type=jnp.float32
    )
    update = lax.all_to_all(
        gelu_value(hidden).astype(jnp.bfloat16), "tensor", split_axis=0, concat_axis=1, tiled=True
    ).astype(jnp.float32)
    out_rows = (xfloat + update).astype(jnp.bfloat16)
    received = shifted(out_rows, "section", 1)
    bfloat, brinv, bnormed = normalize(back_acts[0], gain)
    bnormed_all, bside_all = (
        lax.all_gather(bnormed, "tensor", axis=0, tiled=True),
        lax.all_gather(back_sides[0], "tensor", axis=0, tiled=True),
    )
    bhidden = jnp.dot(bnormed_all, w_top, preferred_element_type=jnp.float32) + jnp.dot(
        bside_all, w_bottom, preferred_element_type=jnp.float32
    )
    grad_cols = lax.all_to_all(back_grads[0], "tensor", split_axis=1, concat_axis=0, tiled=True)
    dhidden = (grad_cols.astype(jnp.float32) * gelu_slope(bhidden)).astype(jnp.bfloat16)
    contract = (((0,), (0,)), ((), ()))
    grad_top = lax.dot_general(bnormed_all, dhidden, contract, preferred_element_type=jnp.float32)
    grad_bottom = lax.dot_general(bside_all, dhidden, contract, preferred_element_type=jnp.float32)
    weight_grads = jnp.concatenate([grad_top, grad_bottom], axis=0).astype(jnp.bfloat16)
    across = (((1,), (1,)), ((), ()))
    dfused = lax.psum_scatter(
        lax.dot_general(dhidden, weight_all, across, preferred_element_type=jnp.float32).astype(
            jnp.bfloat16
        ),
        "tensor",
        scatter_dimension=0,
        tiled=True,
    ).astype(jnp.float32)
    dnormed = dfused[:, :width]
    dside = dfused[:, width:].astype(jnp.bfloat16)
    gain_part = jnp.sum(dnormed * bfloat * brinv, axis=0)
    gain_grad = lax.psum(gain_part, "tensor")
    scaled = gain * dnormed
    dnorm_in = brinv * scaled - bfloat * brinv * brinv * brinv * jnp.mean(
        scaled * bfloat, axis=-1, keepdims=True
    )
    dx_rows = (back_grads[0].astype(jnp.float32) + dnorm_in).astype(jnp.bfloat16)
    grad_received = shifted(dx_rows, "section", -1)
    payload = jnp.where(section_idx < middle, out_rows, dside)
    mirrored = mirror(payload)
    return (
        received[None],
        mirrored[None],
        grad_received[None],
        weight_grads[None],
        gain_grad[None],
    )


def solution(mesh):
    placed = (
        P("section", "tensor", None),
        P("section", "tensor", None),
        P("section", None),
        P("section", None, "tensor"),
        P("section", "tensor", None),
        P("section", "tensor", None),
        P("section", "tensor", None),
    )
    return jax.shard_map(
        on_device,
        mesh=mesh,
        in_specs=placed,
        out_specs=(
            P("section", "tensor", None),
            P("section", "tensor", None),
            P("section", "tensor", None),
            P("section", None, "tensor"),
            P("section", None),
        ),
        check_vma=False,
    )
```

profile of v0, /device:TPU:24, one launch (start us, length us, event | category | flops | bytes accessed | tf_op | source)
XLA Modules:
  0.0 420.0 jit_solution(7512101617935437952)
XLA Ops:
  7.2 0.0 all-gather.9.cloned.1.call-start
  7.2 1.2 fusion.53
  8.4 1.9 fusion.31
  10.3 0.0 all-gather.13.cloned.1.call-start
  10.4 0.7 all-gather.13.cloned.1.call-update
  11.1 1.0 copy.17
  12.1 0.8 copy.13
  12.9 5.7 %all-to-all-start.1 = ((bf16[64,8,384]{2,0,1:T(8,128)(2,1)}), bf16[64,8,384]{2,0,1:T(8,128)(2,1)S(1)}, u32[]{:S(2)}, u32[]{:S(2)}) async-start(bf16[64,8,384]{2,0,1:T(8,128)(2,1)} %copy.13), calls=%async_computation.1 | async-start | bytes 786432 | tf_op jit(solution)/shard_map/all_to_all | solution.py:84
  18.6 41.1 %all-gather.9.cloned.1.call-done = bf16[512,3072]{1,0:T(8,128)(2,1)} async-done(((bf16[64,3072]{1,0:T(8,128)(2,1)}), bf16[512,3072]{1,0:T(8,128)(2,1)}) %all-gather.9.cloned.1.call-update) | async-done | bytes 3145744 | tf_op jit(solution)/shard_map/all_gather | solution.py:78
  59.7 4.4 %fusion.10 = f32[512,384]{1,0:T(8,128)S(1)} fusion(bf16[512,3072]{1,0:T(8,128)(2,1)} %all-gather.9.cloned.1.call-done, bf16[1,6144,384]{2,1,0:T(8,128)(2,1)} %param.10), kind=kOutput, calls=%fused_computation.14 | convolution fusion | flops 1207959552 | bytes 6291456 | tf_op jit(solution)/shard_map/dot_general | solution.py:81
  64.1 43.7 %all-gather.13.cloned.1.call-done = bf16[1,512,3072]{2,1,0:T(8,128)(2,1)} async-done(((bf16[1,64,3072]{2,1,0:T(8,128)(2,1)}), bf16[1,512,3072]{2,1,0:T(8,128)(2,1)}) %all-gather.13.cloned.1.call-update) | async-done | bytes 3145744 | tf_op jit(solution)/shard_map/all_gather | solution.py:79
  107.9 4.9 %fusion.48 = bf16[512,384]{1,0:T(8,128)(2,1)S(1)} fusion(f32[512,384]{1,0:T(8,128)S(1)} %fusion.10, bf16[1,6144,384]{2,1,0:T(8,128)(2,1)} %param.10, bf16[1,512,3072]{2,1,0:T(8,128)(2,1)} %all-gather.13.cloned.1.call-done, bf16[64,8,384]{2,0,1:T(8,128)(2,1)S(1)} %all-to-all-done.1), kind=kOutput, calls=%fused_computation.55 | convolution fusion | flops 1212088320 | bytes 7077888 | tf_op jit(solution)/shard_map/dot_general | solution.py:81
  112.7 7.8 %convolution_convert_fusion = bf16[512,6144]{1,0:T(8,128)(2,1)} fusion(bf16[512,384]{1,0:T(8,128)(2,1)S(1)} %fusion.48, bf16[1,6144,384]{2,1,0:T(8,128)(2,1)} %param.10), kind=kOutput, calls=%fused_computation | convolution fusion | flops 2419064832 | bytes 11403264 | tf_op jit(solution)/shard_map/dot_general | solution.py:92
  120.5 0.0 all-gather.7.cloned.1.call-start
  120.6 0.9 copy-done.1
  121.5 0.2 fusion.49
  121.7 74.3 %reduce-scatter.2.cloned.1.call-done = bf16[64,6144]{1,0:T(8,128)(2,1)} async-done(((bf16[512,6144]{1,0:T(8,128)(2,1)}), bf16[64,6144]{1,0:T(8,128)(2,1)}) %reduce-scatter.2.cloned.1.call-update) | async-done | bytes 786448 | tf_op jit(solution)/shard_map/reduce_scatter | solution.py:91
  196.0 1.3 fusion.56
  197.3 2.2 fusion.36
  199.5 0.0 all-gather.11.cloned.1.call-start
  199.6 0.5 all-gather.11.cloned.1.call-update
  200.1 44.9 %all-gather.7.cloned.1.call-done = bf16[512,3072]{1,0:T(8,128)(2,1)} async-done(((bf16[64,3072]{1,0:T(8,128)(2,1)}), bf16[512,3072]{1,0:T(8,128)(2,1)}) %all-gather.7.cloned.1.call-update) | async-done | bytes 3145744 | tf_op jit(solution)/shard_map/all_gather | solution.py:65
  245.0 4.4 %fusion.12 = f32[512,384]{1,0:T(8,128)S(1)} fusion(bf16[512,3072]{1,0:T(8,128)(2,1)} %all-gather.7.cloned.1.call-done, bf16[1,6144,384]{2,1,0:T(8,128)(2,1)} %param.10), kind=kOutput, calls=%fused_computation.16 | convolution fusion | flops 1207959552 | bytes 6291456 | tf_op jit(solution)/shard_map/dot_general | solution.py:68
  249.4 43.6 %all-gather.11.cloned.1.call-done = bf16[1,512,3072]{2,1,0:T(8,128)(2,1)} async-done(((bf16[1,64,3072]{2,1,0:T(8,128)(2,1)}), bf16[1,512,3072]{2,1,0:T(8,128)(2,1)}) %all-gather.11.cloned.1.call-update) | async-done | bytes 3145744 | tf_op jit(solution)/shard_map/all_gather | solution.py:66
  293.0 5.3 %fusion.41 = bf16[512,384]{1,0:T(8,128)(2,1)} fusion(f32[512,384]{1,0:T(8,128)S(1)} %fusion.12, bf16[1,6144,384]{2,1,0:T(8,128)(2,1)} %param.10, bf16[1,512,3072]{2,1,0:T(8,128)(2,1)} %all-gather.11.cloned.1.call-done), kind=kOutput, calls=%fused_computation.48 | convolution fusion | flops 1209925632 | bytes 6684672 | tf_op jit(solution)/shard_map/dot_general | solution.py:68
  298.3 3.8 all-to-all-start
  302.1 7.8 %all-to-all-done = bf16[8,64,384]{2,1,0:T(8,128)(2,1)S(1)} async-done(((bf16[8,64,384]{2,1,0:T(8,128)(2,1)}), bf16[8,64,384]{2,1,0:T(8,128)(2,1)S(1)}, u32[]{:S(2)}, u32[]{:S(2)}) %all-to-all-start) | async-done | bytes 393248 | tf_op jit(solution)/shard_map/all_to_all | solution.py:71
  309.9 0.1 convert_bitcast_fusion
  310.0 0.1 copy.16
  310.0 0.2 slice_select_fusion
  310.2 0.1 collective-permute-start.1
  310.3 1.7 collective-permute-done.1
  312.0 0.8 collective-permute-start.2
  312.8 10.3 %collective-permute-done.2 = bf16[64,3072]{1,0:T(8,128)(2,1)S(1)} collective-permute-done((bf16[64,3072]{1,0:T(8,128)(2,1)S(1)}, bf16[64,3072]{1,0:T(8,128)(2,1)S(1)}, u32[]{:S(2)}, u32[]{:S(2)}) %collective-permute-start.2) | collective-permute-done | bytes 393248 | tf_op jit(solution)/shard_map/ppermute | solution.py:18
  323.2 1.4 collective-permute-start.3
  324.6 10.4 %collective-permute-done.3 = bf16[64,3072]{1,0:T(8,128)(2,1)S(1)} collective-permute-done((bf16[64,3072]{1,0:T(8,128)(2,1)S(1)}, bf16[64,3072]{1,0:T(8,128)(2,1)S(1)}, u32[]{:S(2)}, u32[]{:S(2)}) %collective-permute-start.3) | collective-permute-done | bytes 393248 | tf_op jit(solution)/shard_map/ppermute | solution.py:18
  335.0 2.5 collective-permute-start.4
  337.5 1.9 fusion.2
  339.4 1.9 fusion.1
  341.3 0.1 collective-permute-start.6
  341.3 0.5 collective-permute-start
  341.8 11.9 %collective-permute-done.4 = bf16[64,3072]{1,0:T(8,128)(2,1)S(1)} collective-permute-done((bf16[64,3072]{1,0:T(8,128)(2,1)S(1)}, bf16[64,3072]{1,0:T(8,128)(2,1)S(1)}, u32[]{:S(2)}, u32[]{:S(2)}) %collective-permute-start.4) | collective-permute-done | bytes 393248 | tf_op jit(solution)/shard_map/ppermute | solution.py:18
  353.7 4.8 %collective-permute-start.5 = (bf16[64,3072]{1,0:T(8,128)(2,1)S(1)}, bf16[64,3072]{1,0:T(8,128)(2,1)S(1)}, u32[]{:S(2)}, u32[]{:S(2)}) collective-permute-start(bf16[64,3072]{1,0:T(8,128)(2,1)S(1)} %collective-permute-done.4), channel_id=1, source_target_pairs={{0,128},{128,0},{8,136},{136,8},{16,144},{144,16},{24,152},{152,24... | collective-permute-start | bytes 1179656 | tf_op jit(solution)/shard_map/ppermute | solution.py:18
  358.6 2.7 pad_maximum_fusion
  361.2 50.0 %psum.7 = f32[1,3072]{1,0:T(1,128)} all-reduce(f32[1,3072]{1,0:T(1,128)S(1)} %bitcast.91), channel_id=1, replica_groups=mesh['section'=32,'tensor'=8] {'tensor'}, use_global_device_ids=true, to_apply=%region_5.0 | all-reduce | flops 3072 | bytes 24576 | tf_op jit(solution)/shard_map/psum | solution.py:102
  411.2 0.7 copy.21
  412.0 0.7 copy.22
  412.7 0.7 copy.23
  (24 shorter events, 0.1 us)
Async XLA Ops:
  7.2 52.6 %all-gather.9.cloned.1.call-start = ((), (), s32[]{:S(2)}) async-start(), calls=%async_computation.4 | async-start | bytes 3538944 | tf_op jit(solution)/shard_map/all_gather | solution.py:78
  10.3 97.5 %all-gather.13.cloned.1.call-start = ((), (), s32[]{:S(2)}) async-start(), calls=%async_computation.7 | async-start | bytes 3538944 | tf_op jit(solution)/shard_map/all_gather | solution.py:79
  12.9 51.2 %all-to-all-start.1 = ((bf16[64,8,384]{2,0,1:T(8,128)(2,1)}), bf16[64,8,384]{2,0,1:T(8,128)(2,1)S(1)}, u32[]{:S(2)}, u32[]{:S(2)}) async-start(bf16[64,8,384]{2,0,1:T(8,128)(2,1)} %copy.13), calls=%async_computation.1 | async-start | bytes 786432 | tf_op jit(solution)/shard_map/all_to_all | solution.py:84
  18.6 177.4 %reduce-scatter.2.cloned.1.call-start = ((), (), s32[]{:S(2)}) async-start(), calls=%async_computation.5 | async-start | bytes 7077888 | tf_op jit(solution)/shard_map/reduce_scatter | solution.py:91
  120.5 1.0 copy-start.1
  120.5 75.5 %copy-start = (bf16[1,64,3072]{2,1,0:T(8,128)(2,1)S(1)}, bf16[1,64,3072]{2,1,0:T(8,128)(2,1)}, u32[]{:S(2)}) copy-start(bf16[1,64,3072]{2,1,0:T(8,128)(2,1)} %param.11) | copy-start | bytes 1179652
  120.5 75.5 %copy-start.4 = (f32[1,3072]{1,0:T(1,128)S(1)}, f32[1,3072]{1,0:T(1,128)}, u32[]{:S(2)}) copy-start(f32[1,3072]{1,0:T(1,128)} %param.9) | copy-start | bytes 36868
  120.5 76.8 %copy-start.3 = (bf16[1,64,3072]{2,1,0:T(8,128)(2,1)S(1)}, bf16[1,64,3072]{2,1,0:T(8,128)(2,1)}, u32[]{:S(2)}) copy-start(bf16[1,64,3072]{2,1,0:T(8,128)(2,1)} %param.13) | copy-start | bytes 1179652
  120.5 124.5 %all-gather.7.cloned.1.call-start = ((), (), s32[]{:S(2)}) async-start(), calls=%async_computation.3 | async-start | bytes 3538944 | tf_op jit(solution)/shard_map/all_gather | solution.py:65
  199.5 93.4 %all-gather.11.cloned.1.call-start = ((), (), s32[]{:S(2)}) async-start(), calls=%async_computation.6 | async-start | bytes 3538944 | tf_op jit(solution)/shard_map/all_gather | solution.py:66
  298.3 11.7 %copy-start.2 = (bf16[64,6144]{1,0:T(8,128)(2,1)S(1)}, bf16[64,6144]{1,0:T(8,128)(2,1)}, u32[]{:S(2)}) copy-start(bf16[64,6144]{1,0:T(8,128)(2,1)} %reduce-scatter.2.cloned.1.call-done) | copy-start | bytes 2359300
  298.3 11.6 %all-to-all-start = ((bf16[8,64,384]{2,1,0:T(8,128)(2,1)}), bf16[8,64,384]{2,1,0:T(8,128)(2,1)S(1)}, u32[]{:S(2)}, u32[]{:S(2)}) async-start(bf16[8,64,384]{2,1,0:T(8,128)(2,1)} %bitcast.6), calls=%async_computation | async-start | bytes 786432 | tf_op jit(solution)/shard_map/all_to_all | solution.py:71
  309.9 27.6 %copy-start.6 = (bf16[1,512,3072]{2,1,0:T(8,128)(2,1)S(1)}, bf16[1,512,3072]{2,1,0:T(8,128)(2,1)}, u32[]{:S(2)}) copy-start(bf16[1,512,3072]{2,1,0:T(8,128)(2,1)} %all-gather.13.cloned.1.call-done) | copy-start | bytes 9437188
  310.2 29.2 %copy-start.5 = (bf16[512,3072]{1,0:T(8,128)(2,1)S(1)}, bf16[512,3072]{1,0:T(8,128)(2,1)}, u32[]{:S(2)}) copy-start(bf16[512,3072]{1,0:T(8,128)(2,1)} %all-gather.9.cloned.1.call-done) | copy-start | bytes 9437188
  310.2 1.8 collective-permute-start.1
  312.0 11.2 %collective-permute-start.2 = (bf16[64,3072]{1,0:T(8,128)(2,1)S(1)}, bf16[64,3072]{1,0:T(8,128)(2,1)S(1)}, u32[]{:S(2)}, u32[]{:S(2)}) collective-permute-start(bf16[64,3072]{1,0:T(8,128)(2,1)S(1)} %collective-permute-done.1), channel_id=1, source_target_pairs={{0,16},{16,0},{8,24},{24,8},{32,48},{48,32},{40,56},{56,40},{64,80... | collective-permute-start | bytes 1179656 | tf_op jit(solution)/shard_map/ppermute | solution.py:18
  323.2 11.8 %collective-permute-start.3 = (bf16[64,3072]{1,0:T(8,128)(2,1)S(1)}, bf16[64,3072]{1,0:T(8,128)(2,1)S(1)}, u32[]{:S(2)}, u32[]{:S(2)}) collective-permute-start(bf16[64,3072]{1,0:T(8,128)(2,1)S(1)} %collective-permute-done.2), channel_id=1, source_target_pairs={{0,32},{32,0},{8,40},{40,8},{16,48},{48,16},{24,56},{56,24},{64,96... | collective-permute-start | bytes 1179656 | tf_op jit(solution)/shard_map/ppermute | solution.py:18
  335.0 18.8 %collective-permute-start.4 = (bf16[64,3072]{1,0:T(8,128)(2,1)S(1)}, bf16[64,3072]{1,0:T(8,128)(2,1)S(1)}, u32[]{:S(2)}, u32[]{:S(2)}) collective-permute-start(bf16[64,3072]{1,0:T(8,128)(2,1)S(1)} %collective-permute-done.3), channel_id=1, source_target_pairs={{0,64},{64,0},{8,72},{72,8},{16,80},{80,16},{24,88},{88,24},{32,96... | collective-permute-start | bytes 1179656 | tf_op jit(solution)/shard_map/ppermute | solution.py:18
  341.3 70.0 %collective-permute-start.6 = (bf16[64,3072]{1,0:T(8,128)(2,1)S(1)}, bf16[64,3072]{1,0:T(8,128)(2,1)S(1)}, u32[]{:S(2)}, u32[]{:S(2)}) collective-permute-start(bf16[64,3072]{1,0:T(8,128)(2,1)S(1)} %get-tuple-element.9), channel_id=1, source_target_pairs={{8,0},{16,8},{24,16},{32,24},{40,32},{48,40},{56,48},{64,56},{72,6... | collective-permute-start | bytes 1179656 | tf_op jit(solution)/shard_map/ppermute | solution.py:24
  341.3 69.9 %collective-permute-start = (bf16[64,3072]{1,0:T(8,128)(2,1)S(1)}, bf16[64,3072]{1,0:T(8,128)(2,1)S(1)}, u32[]{:S(2)}, u32[]{:S(2)}) collective-permute-start(bf16[64,3072]{1,0:T(8,128)(2,1)S(1)} %get-tuple-element.8), channel_id=1, source_target_pairs={{248,0},{0,8},{8,16},{16,24},{24,32},{32,40},{40,48},{48,56},{56,6... | collective-permute-start | bytes 1179656 | tf_op jit(solution)/shard_map/ppermute | solution.py:24
  353.7 57.5 %collective-permute-start.5 = (bf16[64,3072]{1,0:T(8,128)(2,1)S(1)}, bf16[64,3072]{1,0:T(8,128)(2,1)S(1)}, u32[]{:S(2)}, u32[]{:S(2)}) collective-permute-start(bf16[64,3072]{1,0:T(8,128)(2,1)S(1)} %collective-permute-done.4), channel_id=1, source_target_pairs={{0,128},{128,0},{8,136},{136,8},{16,144},{144,16},{24,152},{152,24... | collective-permute-start | bytes 1179656 | tf_op jit(solution)/shard_map/ppermute | solution.py:18
Sparse Core Ops, SparseCore 0:
  10.5 49.2 all-gather.8
  61.5 46.2 all-gather.12
  120.7 75.2 reduce-scatter.1
  199.6 45.3 all-gather.6
  246.6 46.2 all-gather.10
where the time goes:
time: 421 us; the launch traced here: 420 us
  waiting for transfers between devices  291 us (69%)
  blocking collectives  50 us (12%)
  matrix products  30.5 us (7%)
  starting transfers between devices  20 us (5%)
  between operations  13.9 us (3%)
  other arithmetic  9.67 us (2%)
  local copies, waits for them, and re-layouts  5.07 us (1%)
    reduce_scatter x1, waiting for transfers between devices, on_device(): lax.psum_scatter(lax.dot_general(dhidden, weight_all, across, preferred_e...  74.3 us
    psum x1, blocking collectives, on_device(): gain_grad = lax.psum(gain_part, 'tensor')  50 us
    all_gather x1, waiting for transfers between devices, on_device(): lax.all_gather(normed, 'tensor', axis=0, tiled=True)  44.9 us
    all_gather x1, waiting for transfers between devices, on_device(): lax.all_gather(back_sides[0], 'tensor', axis=0, tiled=True)  43.7 us
    all_gather x1, waiting for transfers between devices, on_device(): lax.all_gather(sides[0], 'tensor', axis=0, tiled=True)  43.6 us
    all_gather x1, waiting for transfers between devices, on_device(): lax.all_gather(bnormed, 'tensor', axis=0, tiled=True)  41.1 us
    ppermute x5, waiting for transfers between devices, swapped(): return lax.ppermute(block, axis, route)  34.3 us
    ppermute x5, starting transfers between devices, swapped(): return lax.ppermute(block, axis, route)  9.73 us
  transfers between devices with their start and end apart: 14, of which 10 were waited for; matrix products, arithmetic and copies ran while one was open for 4% of the time, Pallas kernels for 0%

commit v1 on v0

--- a/solution.py
+++ b/solution.py
@@ -2,10 +2,17 @@
 import jax.numpy as jnp
 from jax import lax
 from jax.sharding import PartitionSpec as P
+from jax.lax import all_to_all, axis_size
 
 epsilon = 1e-06
 tanh_scale = 0.7978845608028654
 cubic_term = 0.044715
+
+
+def _cut_halves(values):
+    part_next = axis_size("tensor")
+    tmp = jnp.stack([values] * part_next, 0)
+    return jnp.concatenate(all_to_all(tmp, axis_name="tensor", split_axis=0, concat_axis=0), axis=0)
 
 
 def swapped(block, axis, apart):
@@ -76,7 +83,7 @@
     bfloat, brinv, bnormed = normalize(back_acts[0], gain)
     bnormed_all, bside_all = (
         lax.all_gather(bnormed, "tensor", axis=0, tiled=True),
-        lax.all_gather(back_sides[0], "tensor", axis=0, tiled=True),
+        _cut_halves(back_sides[0]),
     )
     bhidden = jnp.dot(bnormed_all, w_top, preferred_element_type=jnp.float32) + jnp.dot(
         bside_all, w_bottom, preferred_element_type=jnp.float32

time: 421 us -> 403 us (0.957)
  waiting for transfers between devices: 291 us -> 267 us
  starting transfers between devices: 20 us -> 24.8 us
    all_to_all x0 -> x1, waiting for transfers between devices: none -> 48.2 us  [_cut_halves(): all_to_all(tmp, axis_name='tensor', split_axis=0, concat_axis=0)]
    all_gather x1 -> x0, waiting for transfers between devices: 43.7 us -> none  [on_device(): lax.all_gather(back_sides[0], 'tensor', axis=0, tiled=True)]
    all_gather x1, waiting for transfers between devices: 41.1 us -> 4.79 us  [on_device(): lax.all_gather(bnormed, 'tensor', axis=0, tiled=True)]
    all_to_all x1, waiting for transfers between devices: 0.01 us -> 8.85 us  [on_device(): lax.all_to_all(back_grads[0], 'tensor', split_axis=1, concat_axis=0, tile...]
    all_to_all x0 -> x1, starting transfers between devices: none -> 5.79 us  [_cut_halves(): all_to_all(tmp, axis_name='tensor', split_axis=0, concat_axis=0)]
  transfers between devices with their start and end apart: 14 -> 14, of which waited for: 10 -> 11; matrix products, arithmetic and copies ran while one was open for 4% -> 5% of each run, Pallas kernels for 0% -> 0%
where the time goes in v1:
time: 403 us; the launch traced here: 402 us
  waiting for transfers between devices  267 us (66%)
  blocking collectives  49.8 us (12%)
  matrix products  32.4 us (8%)
  starting transfers between devices  24.8 us (6%)
  between operations  13.9 us (3%)
  other arithmetic  7.68 us (2%)
  local copies, waits for them, and re-layouts  7.12 us (2%)
    reduce_scatter x1, waiting for transfers between devices, on_device(): lax.psum_scatter(lax.dot_general(dhidden, weight_all, across, preferred_e...  75.4 us
    psum x1, blocking collectives, on_device(): gain_grad = lax.psum(gain_part, 'tensor')  49.8 us
    all_to_all x1, waiting for transfers between devices, _cut_halves(): all_to_all(tmp, axis_name='tensor', split_axis=0, concat_axis=0)  48.2 us
    all_gather x1, waiting for transfers between devices, on_device(): lax.all_gather(normed, 'tensor', axis=0, tiled=True)  44.9 us
    all_gather x1, waiting for transfers between devices, on_device(): lax.all_gather(sides[0], 'tensor', axis=0, tiled=True)  43.6 us
    ppermute x5, waiting for transfers between devices, swapped(): return lax.ppermute(block, axis, route)  32.4 us
    ppermute x5, starting transfers between devices, swapped(): return lax.ppermute(block, axis, route)  9.73 us
    all_to_all x1, waiting for transfers between devices, on_device(): lax.all_to_all(back_grads[0], 'tensor', split_axis=1, concat_axis=0, tile...  8.85 us
  transfers between devices with their start and end apart: 14, of which 11 were waited for; matrix products, arithmetic and copies ran while one was open for 5% of the time, Pallas kernels for 0%

profile of v1, /device:TPU:24, one launch (start us, length us, event | category | flops | bytes accessed | tf_op | source)
XLA Modules:
  0.0 402.3 jit_solution(692399063254372523)
XLA Ops:
  7.2 3.0 stack.3
  10.2 5.8 %all-to-all-start.2 = ((bf16[8,64,3072]{2,1,0:T(8,128)(2,1)}), bf16[8,64,3072]{2,1,0:T(8,128)(2,1)}, u32[]{:S(2)}, u32[]{:S(2)}) async-start(bf16[8,64,3072]{2,1,0:T(8,128)(2,1)} %stack.3), calls=%async_computation.2 | async-start | bytes 6291456 | tf_op jit(solution)/shard_map/all_to_all | solution.py:15
  16.1 0.2 fusion.49
  16.3 0.9 fusion.27
  17.3 0.8 copy.13
  18.0 48.2 %all-to-all-done.2 = bf16[8,64,3072]{2,1,0:T(8,128)(2,1)} async-done(((bf16[8,64,3072]{2,1,0:T(8,128)(2,1)}), bf16[8,64,3072]{2,1,0:T(8,128)(2,1)}, u32[]{:S(2)}, u32[]{:S(2)}) %all-to-all-start.2) | async-done | bytes 3145760 | tf_op jit(solution)/shard_map/all_to_all | solution.py:15
  66.3 4.8 %all-to-all-start.1 = ((bf16[64,8,384]{2,0,1:T(8,128)(2,1)}), bf16[64,8,384]{2,0,1:T(8,128)(2,1)S(1)}, u32[]{:S(2)}, u32[]{:S(2)}) async-start(bf16[64,8,384]{2,0,1:T(8,128)(2,1)} %copy.13), calls=%async_computation.1 | async-start | bytes 786432 | tf_op jit(solution)/shard_map/all_to_all | solution.py:91
  71.0 0.0 reduce-scatter.2.cloned.1.call-start
  71.1 4.5 %fusion.5 = f32[512,384]{1,0:T(8,128)S(1)} fusion(bf16[512,3072]{1,0:T(8,128)(2,1)} %bitcast.14, bf16[1,6144,384]{2,1,0:T(8,128)(2,1)} %param.10), kind=kOutput, calls=%fused_computation.9 | convolution fusion | flops 1207959552 | bytes 6291456 | tf_op jit(solution)/shard_map/dot_general | solution.py:88
  75.6 8.9 %all-to-all-done.1 = bf16[64,8,384]{2,0,1:T(8,128)(2,1)S(1)} async-done(((bf16[64,8,384]{2,0,1:T(8,128)(2,1)}), bf16[64,8,384]{2,0,1:T(8,128)(2,1)S(1)}, u32[]{:S(2)}, u32[]{:S(2)}) %all-to-all-start.1) | async-done | bytes 393248 | tf_op jit(solution)/shard_map/all_to_all | solution.py:91
  84.4 4.8 %all-gather.7.cloned.1.call-done = bf16[512,3072]{1,0:T(8,128)(2,1)} async-done(((bf16[64,3072]{1,0:T(8,128)(2,1)}), bf16[512,3072]{1,0:T(8,128)(2,1)}) %all-gather.7.cloned.1.call-update) | async-done | bytes 3145744 | tf_op jit(solution)/shard_map/all_gather | solution.py:85
  89.2 4.9 %fusion.44 = bf16[512,384]{1,0:T(8,128)(2,1)S(1)} fusion(f32[512,384]{1,0:T(8,128)S(1)} %fusion.5, bf16[512,3072]{1,0:T(8,128)(2,1)} %all-gather.7.cloned.1.call-done, bf16[1,6144,384]{2,1,0:T(8,128)(2,1)} %param.10, bf16[64,8,384]{2,0,1:T(8,128)(2,1)S(1)} %all-to-all-done.1), kind=kOutput, calls=%fused_computation.53 | convolution fusion | flops 1212088320 | bytes 7077888 | tf_op jit(solution)/shard_map/dot_general | solution.py:88
  94.1 7.8 %convolution_convert_fusion = bf16[512,6144]{1,0:T(8,128)(2,1)} fusion(bf16[512,384]{1,0:T(8,128)(2,1)S(1)} %fusion.44, bf16[1,6144,384]{2,1,0:T(8,128)(2,1)} %param.10), kind=kOutput, calls=%fused_computation | convolution fusion | flops 2419064832 | bytes 11403264 | tf_op jit(solution)/shard_map/dot_general | solution.py:99
  101.9 0.0 all-gather.5.cloned.1.call-start
  101.9 0.9 copy-done.1
  102.8 0.2 fusion.45
  103.0 75.4 %reduce-scatter.2.cloned.1.call-done = bf16[64,6144]{1,0:T(8,128)(2,1)} async-done(((bf16[512,6144]{1,0:T(8,128)(2,1)}), bf16[64,6144]{1,0:T(8,128)(2,1)}) %reduce-scatter.2.cloned.1.call-update) | async-done | bytes 786448 | tf_op jit(solution)/shard_map/reduce_scatter | solution.py:98
  178.5 1.3 fusion.52
  179.8 2.2 fusion.32
  182.0 0.0 all-gather.9.cloned.1.call-start
  182.1 0.5 all-gather.9.cloned.1.call-update
  182.6 44.9 %all-gather.5.cloned.1.call-done = bf16[512,3072]{1,0:T(8,128)(2,1)} async-done(((bf16[64,3072]{1,0:T(8,128)(2,1)}), bf16[512,3072]{1,0:T(8,128)(2,1)}) %all-gather.5.cloned.1.call-update) | async-done | bytes 3145744 | tf_op jit(solution)/shard_map/all_gather | solution.py:72
  227.5 4.4 %fusion.10 = f32[512,384]{1,0:T(8,128)S(1)} fusion(bf16[512,3072]{1,0:T(8,128)(2,1)} %all-gather.5.cloned.1.call-done, bf16[1,6144,384]{2,1,0:T(8,128)(2,1)} %param.10), kind=kOutput, calls=%fused_computation.14 | convolution fusion | flops 1207959552 | bytes 6291456 | tf_op jit(solution)/shard_map/dot_general | solution.py:75
  231.9 43.6 %all-gather.9.cloned.1.call-done = bf16[1,512,3072]{2,1,0:T(8,128)(2,1)} async-done(((bf16[1,64,3072]{2,1,0:T(8,128)(2,1)}), bf16[1,512,3072]{2,1,0:T(8,128)(2,1)}) %all-gather.9.cloned.1.call-update) | async-done | bytes 3145744 | tf_op jit(solution)/shard_map/all_gather | solution.py:73
  275.5 5.3 %fusion.37 = bf16[512,384]{1,0:T(8,128)(2,1)} fusion(f32[512,384]{1,0:T(8,128)S(1)} %fusion.10, bf16[1,6144,384]{2,1,0:T(8,128)(2,1)} %param.10, bf16[1,512,3072]{2,1,0:T(8,128)(2,1)} %all-gather.9.cloned.1.call-done), kind=kOutput, calls=%fused_computation.46 | convolution fusion | flops 1209925632 | bytes 6684672 | tf_op jit(solution)/shard_map/dot_general | solution.py:75
  280.8 3.8 all-to-all-start
  284.7 7.8 %all-to-all-done = bf16[8,64,384]{2,1,0:T(8,128)(2,1)S(1)} async-done(((bf16[8,64,384]{2,1,0:T(8,128)(2,1)}), bf16[8,64,384]{2,1,0:T(8,128)(2,1)S(1)}, u32[]{:S(2)}, u32[]{:S(2)}) %all-to-all-start) | async-done | bytes 393248 | tf_op jit(solution)/shard_map/all_to_all | solution.py:78
  292.4 0.1 convert_bitcast_fusion
  292.5 0.1 copy.16
  292.6 0.2 slice_select_fusion
  292.7 0.1 collective-permute-start.1
  292.8 1.7 collective-permute-done.1
  294.5 0.8 collective-permute-start.2
  295.4 10.3 %collective-permute-done.2 = bf16[64,3072]{1,0:T(8,128)(2,1)S(1)} collective-permute-done((bf16[64,3072]{1,0:T(8,128)(2,1)S(1)}, bf16[64,3072]{1,0:T(8,128)(2,1)S(1)}, u32[]{:S(2)}, u32[]{:S(2)}) %collective-permute-start.2) | collective-permute-done | bytes 393248 | tf_op jit(solution)/shard_map/ppermute | solution.py:25
  305.7 1.4 collective-permute-start.3
  307.1 10.4 %collective-permute-done.3 = bf16[64,3072]{1,0:T(8,128)(2,1)S(1)} collective-permute-done((bf16[64,3072]{1,0:T(8,128)(2,1)S(1)}, bf16[64,3072]{1,0:T(8,128)(2,1)S(1)}, u32[]{:S(2)}, u32[]{:S(2)}) %collective-permute-start.3) | collective-permute-done | bytes 393248 | tf_op jit(solution)/shard_map/ppermute | solution.py:25
  317.5 2.5 collective-permute-start.4
  320.1 3.7 fusion.2
  323.8 1.9 fusion.1
  325.7 0.1 collective-permute-start.6
  325.8 0.5 collective-permute-start
  326.3 10.0 %collective-permute-done.4 = bf16[64,3072]{1,0:T(8,128)(2,1)S(1)} collective-permute-done((bf16[64,3072]{1,0:T(8,128)(2,1)S(1)}, bf16[64,3072]{1,0:T(8,128)(2,1)S(1)}, u32[]{:S(2)}, u32[]{:S(2)}) %collective-permute-start.4) | collective-permute-done | bytes 393248 | tf_op jit(solution)/shard_map/ppermute | solution.py:25
  336.3 4.8 %collective-permute-start.5 = (bf16[64,3072]{1,0:T(8,128)(2,1)S(1)}, bf16[64,3072]{1,0:T(8,128)(2,1)S(1)}, u32[]{:S(2)}, u32[]{:S(2)}) collective-permute-start(bf16[64,3072]{1,0:T(8,128)(2,1)S(1)} %collective-permute-done.4), channel_id=1, source_target_pairs={{0,128},{128,0},{8,136},{136,8},{16,144},{144,16},{24,152},{152,24... | collective-permute-start | bytes 1179656 | tf_op jit(solution)/shard_map/ppermute | solution.py:25
  341.1 2.7 pad_maximum_fusion
  343.8 49.8 %psum.7 = f32[1,3072]{1,0:T(1,128)} all-reduce(f32[1,3072]{1,0:T(1,128)S(1)} %bitcast.87), channel_id=1, replica_groups=mesh['section'=32,'tensor'=8] {'tensor'}, use_global_device_ids=true, to_apply=%region_5.0 | all-reduce | flops 3072 | bytes 24576 | tf_op jit(solution)/shard_map/psum | solution.py:109
  393.5 0.7 copy.21
  394.3 0.7 copy.22
  395.0 0.7 copy.23
  (22 shorter events, 0.2 us)
Async XLA Ops:
  10.2 5.8 %copy-start = (bf16[1,64,3072]{2,1,0:T(8,128)(2,1)S(1)}, bf16[1,64,3072]{2,1,0:T(8,128)(2,1)}, u32[]{:S(2)}) copy-start(bf16[1,64,3072]{2,1,0:T(8,128)(2,1)} %param.11) | copy-start | bytes 1179652
  10.2 6.0 %copy-start.4 = (f32[1,3072]{1,0:T(1,128)S(1)}, f32[1,3072]{1,0:T(1,128)}, u32[]{:S(2)}) copy-start(f32[1,3072]{1,0:T(1,128)} %param.9) | copy-start | bytes 36868
  10.2 7.0 %copy-start.3 = (bf16[1,64,3072]{2,1,0:T(8,128)(2,1)S(1)}, bf16[1,64,3072]{2,1,0:T(8,128)(2,1)}, u32[]{:S(2)}) copy-start(bf16[1,64,3072]{2,1,0:T(8,128)(2,1)} %param.13) | copy-start | bytes 1179652
  10.2 56.1 %all-to-all-start.2 = ((bf16[8,64,3072]{2,1,0:T(8,128)(2,1)}), bf16[8,64,3072]{2,1,0:T(8,128)(2,1)}, u32[]{:S(2)}, u32[]{:S(2)}) async-start(bf16[8,64,3072]{2,1,0:T(8,128)(2,1)} %stack.3), calls=%async_computation.2 | async-start | bytes 6291456 | tf_op jit(solution)/shard_map/all_to_all | solution.py:15
  16.0 73.2 %all-gather.7.cloned.1.call-start = ((), (), s32[]{:S(2)}) async-start(), calls=%async_computation.5 | async-start | bytes 3538944 | tf_op jit(solution)/shard_map/all_gather | solution.py:85
  66.3 18.1 %all-to-all-start.1 = ((bf16[64,8,384]{2,0,1:T(8,128)(2,1)}), bf16[64,8,384]{2,0,1:T(8,128)(2,1)S(1)}, u32[]{:S(2)}, u32[]{:S(2)}) async-start(bf16[64,8,384]{2,0,1:T(8,128)(2,1)} %copy.13), calls=%async_computation.1 | async-start | bytes 786432 | tf_op jit(solution)/shard_map/all_to_all | solution.py:91
  71.0 107.4 %reduce-scatter.2.cloned.1.call-start = ((), (), s32[]{:S(2)}) async-start(), calls=%async_computation.6 | async-start | bytes 7077888 | tf_op jit(solution)/shard_map/reduce_scatter | solution.py:98
  101.8 1.0 copy-start.1
  101.9 125.6 %all-gather.5.cloned.1.call-start = ((), (), s32[]{:S(2)}) async-start(), calls=%async_computation.4 | async-start | bytes 3538944 | tf_op jit(solution)/shard_map/all_gather | solution.py:72
  182.0 93.5 %all-gather.9.cloned.1.call-start = ((), (), s32[]{:S(2)}) async-start(), calls=%async_computation.7 | async-start | bytes 3538944 | tf_op jit(solution)/shard_map/all_gather | solution.py:73
  280.8 11.7 %copy-start.2 = (bf16[64,6144]{1,0:T(8,128)(2,1)S(1)}, bf16[64,6144]{1,0:T(8,128)(2,1)}, u32[]{:S(2)}) copy-start(bf16[64,6144]{1,0:T(8,128)(2,1)} %reduce-scatter.2.cloned.1.call-done) | copy-start | bytes 2359300
  280.8 11.6 %all-to-all-start = ((bf16[8,64,384]{2,1,0:T(8,128)(2,1)}), bf16[8,64,384]{2,1,0:T(8,128)(2,1)S(1)}, u32[]{:S(2)}, u32[]{:S(2)}) async-start(bf16[8,64,384]{2,1,0:T(8,128)(2,1)} %bitcast.6), calls=%async_computation | async-start | bytes 786432 | tf_op jit(solution)/shard_map/all_to_all | solution.py:78
  292.7 31.1 %copy-start.5 = (bf16[512,3072]{1,0:T(8,128)(2,1)S(1)}, bf16[512,3072]{1,0:T(8,128)(2,1)}, u32[]{:S(2)}) copy-start(bf16[512,3072]{1,0:T(8,128)(2,1)} %all-gather.7.cloned.1.call-done) | copy-start | bytes 9437188
  292.7 1.8 collective-permute-start.1
  294.5 11.2 %collective-permute-start.2 = (bf16[64,3072]{1,0:T(8,128)(2,1)S(1)}, bf16[64,3072]{1,0:T(8,128)(2,1)S(1)}, u32[]{:S(2)}, u32[]{:S(2)}) collective-permute-start(bf16[64,3072]{1,0:T(8,128)(2,1)S(1)} %collective-permute-done.1), channel_id=1, source_target_pairs={{0,16},{16,0},{8,24},{24,8},{32,48},{48,32},{40,56},{56,40},{64,80... | collective-permute-start | bytes 1179656 | tf_op jit(solution)/shard_map/ppermute | solution.py:25
  305.7 11.8 %collective-permute-start.3 = (bf16[64,3072]{1,0:T(8,128)(2,1)S(1)}, bf16[64,3072]{1,0:T(8,128)(2,1)S(1)}, u32[]{:S(2)}, u32[]{:S(2)}) collective-permute-start(bf16[64,3072]{1,0:T(8,128)(2,1)S(1)} %collective-permute-done.2), channel_id=1, source_target_pairs={{0,32},{32,0},{8,40},{40,8},{16,48},{48,16},{24,56},{56,24},{64,96... | collective-permute-start | bytes 1179656 | tf_op jit(solution)/shard_map/ppermute | solution.py:25
  317.5 18.8 %collective-permute-start.4 = (bf16[64,3072]{1,0:T(8,128)(2,1)S(1)}, bf16[64,3072]{1,0:T(8,128)(2,1)S(1)}, u32[]{:S(2)}, u32[]{:S(2)}) collective-permute-start(bf16[64,3072]{1,0:T(8,128)(2,1)S(1)} %collective-permute-done.3), channel_id=1, source_target_pairs={{0,64},{64,0},{8,72},{72,8},{16,80},{80,16},{24,88},{88,24},{32,96... | collective-permute-start | bytes 1179656 | tf_op jit(solution)/shard_map/ppermute | solution.py:25
  325.7 67.9 %collective-permute-start.6 = (bf16[64,3072]{1,0:T(8,128)(2,1)S(1)}, bf16[64,3072]{1,0:T(8,128)(2,1)S(1)}, u32[]{:S(2)}, u32[]{:S(2)}) collective-permute-start(bf16[64,3072]{1,0:T(8,128)(2,1)S(1)} %get-tuple-element.9), channel_id=1, source_target_pairs={{8,0},{16,8},{24,16},{32,24},{40,32},{48,40},{56,48},{64,56},{72,6... | collective-permute-start | bytes 1179656 | tf_op jit(solution)/shard_map/ppermute | solution.py:31
  325.8 67.8 %collective-permute-start = (bf16[64,3072]{1,0:T(8,128)(2,1)S(1)}, bf16[64,3072]{1,0:T(8,128)(2,1)S(1)}, u32[]{:S(2)}, u32[]{:S(2)}) collective-permute-start(bf16[64,3072]{1,0:T(8,128)(2,1)S(1)} %get-tuple-element.8), channel_id=1, source_target_pairs={{248,0},{0,8},{8,16},{16,24},{24,32},{32,40},{40,48},{48,56},{56,6... | collective-permute-start | bytes 1179656 | tf_op jit(solution)/shard_map/ppermute | solution.py:31
  336.3 57.3 %collective-permute-start.5 = (bf16[64,3072]{1,0:T(8,128)(2,1)S(1)}, bf16[64,3072]{1,0:T(8,128)(2,1)S(1)}, u32[]{:S(2)}, u32[]{:S(2)}) collective-permute-start(bf16[64,3072]{1,0:T(8,128)(2,1)S(1)} %collective-permute-done.4), channel_id=1, source_target_pairs={{0,128},{128,0},{8,136},{136,8},{16,144},{144,16},{24,152},{152,24... | collective-permute-start | bytes 1179656 | tf_op jit(solution)/shard_map/ppermute | solution.py:25
Sparse Core Ops, SparseCore 0:
  19.2 69.9 all-gather.6
  102.0 76.4 reduce-scatter.1
  182.1 45.3 all-gather.4
  229.2 46.2 all-gather.8
